TPU v7x, 128 devices: a whole 4x4x4 slice. The times are simulated.
128 devices in a mesh: grp: 4 (over x), gx: 4 (over y), gy: 8 (over z, core).
Axes of the slice: x: 4, y: 4, z: 4, core: 2. Of those that a mesh axis runs over, the one named last changes fastest.
Arguments:
- modes_now: float32 [4, 32, 512, 1024], P('grp', ('gx', 'gy')), may hold values from -6 to 6
- modes_old: float32 [4, 32, 512, 1024], P('grp', ('gx', 'gy')), may hold values from -6 to 6
- pressure_now: float32 [4, 32, 512, 1024], P('grp', None, 'gx', 'gy'), may hold values from -6 to 6
- source: float32 [4, 32, 512, 1024], P('grp', None, 'gx', 'gy'), may hold values from -6 to 6
- strip_slot: int32 [4, 512, 8], P('grp', 'gx', 'gy'), may hold values from 0 to 255, as said below
- strip_row: int32 [4, 512, 8], P('grp', 'gx', 'gy'), may hold values from 0 to 127, as said below
Outputs:
- modes_new: float32 [4, 32, 512, 1024], P('grp', ('gx', 'gy'))
- pressure_next: float32 [4, 32, 512, 1024], P('grp', None, 'gx', 'gy')
Inputs may be any that keep to these rules, and one draw needn't show every extreme that they name: The 128 strips of one device take distinct values of strip_slot. Each device sends to every other device (itself included) either no strip or exactly 2, and every bottom-face strip of every device is met by exactly one top-face strip. `strip_row`: see strip_slot.
All inputs are finite; a program needn't handle non-finite values.
Results may differ from a plain program's by a relative error of at most 0.00007.
Values sent between devices are 32-bit elements; how exact they have to be, the bound alone decides.
No kernel may reach another device: no remote copies, remote signals or barrier semaphores. Data moves between devices by JAX's collectives and lax.ppermute only.
A program may use at most 64 MiB of HBM per device.

v0:
```python
import jax
import jax.numpy as jnp
from jax import lax
from jax.sharding import PartitionSpec as P

COURANT = 0.5
WEIGHTS = (1.5, -0.15, 2.0 / 180.0)
HIGH = lax.Precision.HIGHEST
FAST = lax.Precision.HIGH


def cosine_table(count):
    rows = jnp.arange(count, dtype=jnp.int32).astype(jnp.float32)[:, None]
    cols = jnp.arange(count, dtype=jnp.int32).astype(jnp.float32)[None, :]
    scale = jnp.where(rows == 0, jnp.sqrt(1.0 / count), jnp.sqrt(2.0 / count))
    return scale * jnp.cos(jnp.pi * rows * (cols + 0.5) / count)


def face_stencil(diff):
    first = diff[..., 0, :]
    second = diff[..., 1, :]
    third = diff[..., 2, :]
    return jnp.stack(
        [
            WEIGHTS[0] * first + WEIGHTS[1] * second + WEIGHTS[2] * third,
            WEIGHTS[1] * first + WEIGHTS[2] * second,
            WEIGHTS[2] * first,
        ],
        axis=-2,
    )


def to_modes(field, table_z, table_x, table_y):
    width_x = lax.axis_size("gx")
    width_y = lax.axis_size("gy")
    rows_x = field.shape[2]
    cols_y = field.shape[3]
    part = jnp.einsum("kz,zxy->kxy", table_z, field[0], precision=HIGH)
    part = lax.all_to_all(part, ("gx", "gy"), split_axis=0, concat_axis=0, tiled=True)
    part = part.reshape(width_x, width_y, rows_x, cols_y)
    split_x = table_x.reshape(table_x.shape[0], width_x, rows_x)
    split_y = table_y.reshape(table_y.shape[0], width_y, cols_y)
    part = jnp.einsum("bix,ijxy->bjy", split_x, part, precision=FAST)
    return jnp.einsum("cjy,bjy->bc", split_y, part, precision=FAST)[None, None]


def to_cells(modes, table_z, table_x, table_y):
    width_x = lax.axis_size("gx")
    width_y = lax.axis_size("gy")
    rows_x = modes.shape[2] // width_x
    cols_y = modes.shape[3] // width_y
    split_x = table_x.reshape(table_x.shape[0], width_x, rows_x)
    split_y = table_y.reshape(table_y.shape[0], width_y, cols_y)
    part = jnp.einsum("cjy,bc->bjy", split_y, modes[0, 0], precision=FAST)
    part = jnp.einsum("bix,bjy->ijxy", split_x, part, precision=FAST)
    part = part.reshape(width_x * width_y, rows_x, cols_y)
    cells = lax.all_to_all(part, ("gx", "gy"), split_axis=0, concat_axis=0, tiled=True)
    return jnp.einsum("kz,kxy->zxy", table_z, cells, precision=HIGH)[None]


def advance_terms(depth_index, depth, long_x, long_y):
    index_x = jnp.arange(long_x, dtype=jnp.int32).astype(jnp.float32)
    index_y = jnp.arange(long_y, dtype=jnp.int32).astype(jnp.float32)
    part_z = depth_index / depth * (depth_index / depth)
    part_x = index_x / long_x * (index_x / long_x)
    part_y = index_y / long_y * (index_y / long_y)
    theta = (
        COURANT
        * jnp.pi
        * jnp.sqrt(part_z[:, None, None] + part_x[None, :, None] + part_y[None, None, :])
    )
    shape = jnp.sinc(theta / (2.0 * jnp.pi))
    return (2.0 * jnp.cos(theta), COURANT * COURANT * shape * shape)


def lane_stencil(diff, cols):
    first = diff[:, :cols]
    second = diff[:, cols : 2 * cols]
    third = diff[:, 2 * cols :]
    return jnp.concatenate(
        [
            WEIGHTS[0] * first + WEIGHTS[1] * second + WEIGHTS[2] * third,
            WEIGHTS[1] * first + WEIGHTS[2] * second,
            WEIGHTS[2] * first,
        ],
        axis=1,
    )


def one_hot(index, count):
    return (index[:, None] == jnp.arange(count, dtype=jnp.int32)[None, :]).astype(jnp.float32)


def shards(modes_now, modes_old, pressure_now, source, strip_slot, strip_row):
    depth = source.shape[1]
    rows_x = source.shape[2]
    cols_y = source.shape[3]
    planes = modes_now.shape[1]
    long_x = modes_now.shape[2]
    long_y = modes_now.shape[3]
    block = lax.axis_index(("gx", "gy"))
    depth_index = (block * planes + jnp.arange(planes, dtype=jnp.int32)).astype(jnp.float32)
    table_z = lax.optimization_barrier(cosine_table(depth))
    table_x = lax.optimization_barrier(cosine_table(long_x))
    table_y = lax.optimization_barrier(cosine_table(long_y))
    scale_now, scale_spec = advance_terms(depth_index, depth, long_x, long_y)
    scale_now = lax.optimization_barrier(scale_now)
    scale_spec = lax.optimization_barrier(scale_spec)
    top = jnp.stack(
        [pressure_now[0, depth - 1], pressure_now[0, depth - 2], pressure_now[0, depth - 3]], axis=1
    ).reshape(rows_x, 3 * cols_y)
    bottom = jnp.transpose(pressure_now[0, 0:3], (1, 0, 2)).reshape(rows_x, 3 * cols_y)
    every = ("grp", "gx", "gy")
    devices = lax.axis_size(every)
    slots_per = max(2, rows_x // devices)
    total = devices * slots_per
    slots = strip_slot.reshape(-1)
    mine = (slots * rows_x + strip_row.reshape(-1)).astype(jnp.float32)
    owner = jnp.arange(devices, dtype=jnp.int32)[:, None] == lax.axis_index(every)
    codes = lax.psum(jnp.where(owner, mine[None, :], 0.0), every)
    codes = jnp.round(codes).astype(jnp.int32)
    want = lax.axis_index(every) * slots_per + jnp.arange(slots_per, dtype=jnp.int32)
    hit = (codes // rows_x)[:, :, None] == want[None, None, :]
    found = jnp.any(hit, axis=1).reshape(total)
    marks = jnp.sum(jnp.where(hit, (codes % rows_x)[:, :, None], 0), axis=1).reshape(total)
    marks = jnp.where(found, marks, -1)
    send = one_hot(slots, total)
    meet = one_hot(marks, rows_x)
    rims_out = jnp.einsum("sk,sf->kf", send, top, precision=HIGH)
    met = jnp.einsum("kr,rf->kf", meet, bottom, precision=HIGH)
    got = lax.all_to_all(
        jnp.concatenate([rims_out, met], axis=1), every, split_axis=0, concat_axis=0, tiled=True
    )
    rims = got[:, : 3 * cols_y]
    far = got[:, 3 * cols_y :]
    live = found.astype(jnp.float32)[:, None]
    force = lane_stencil(met - rims, cols_y) * live
    bottom_force = jnp.einsum("kr,kf->rf", meet, -force, precision=HIGH).reshape(rows_x, 3, cols_y)
    partner = jnp.einsum("sk,kf->sf", send, far, precision=HIGH)
    top_force = lane_stencil(partner - top, cols_y).reshape(rows_x, 3, cols_y)
    forcing = source.at[:, 0:3].add(jnp.transpose(bottom_force, (1, 0, 2))[None])
    forcing = forcing.at[:, depth - 1].add(top_force[:, 0][None])
    forcing = forcing.at[:, depth - 2].add(top_force[:, 1][None])
    forcing = forcing.at[:, depth - 3].add(top_force[:, 2][None])
    spectrum = to_modes(forcing, table_z, table_x, table_y)
    modes_new = (scale_now * modes_now[0] - modes_old[0] + scale_spec * spectrum[0])[None]
    pressure_next = to_cells(modes_new, table_z, table_x, table_y)
    return (modes_new, pressure_next)


def solution(mesh):
    placed = (
        P("grp", ("gx", "gy"), None, None),
        P("grp", ("gx", "gy"), None, None),
        P("grp", None, "gx", "gy"),
        P("grp", None, "gx", "gy"),
        P("grp", "gx", "gy"),
        P("grp", "gx", "gy"),
    )
    return jax.shard_map(
        shards,
        mesh=mesh,
        in_specs=placed,
        out_specs=(P("grp", ("gx", "gy"), None, None), P("grp", None, "gx", "gy")),
        check_vma=False,
    )
```

profile of v0, /device:TPU:1, one launch (start us, length us, event | category | flops | bytes accessed | tf_op | source)
XLA Modules:
  0.0 294.6 jit_solution(2548714859366596820)
XLA Ops:
  7.2 0.0 slice-start
  7.2 0.0 all-reduce.2.cloned.1.call-start
  7.2 0.7 fusion.64
  8.0 0.7 broadcast_select_fusion
  8.7 0.0 all-reduce.2.cloned.1.call-update
  8.7 0.9 fusion.66
  9.6 0.1 copy.109
  9.7 0.1 copy.110
  9.8 0.1 copy.111
  9.9 1.1 fusion.43
  11.0 0.0 slice-done
  11.1 0.1 copy.108
  11.2 145.1 %all-reduce.2.cloned.1.call-done = f32[128,128]{1,0:T(8,128)} async-done(((f32[128,128]{1,0:T(8,128)}), f32[128,128]{1,0:T(8,128)}) %all-reduce.2.cloned.1.call-update) | async-done | bytes 65552 | tf_op jit(solution)/shard_map/psum | solution.py:120
  156.3 0.9 add_select_fusion
  157.2 0.2 compare_reduce_fusion
  157.4 0.2 fusion.39
  157.6 0.1 copy.74
  157.7 0.1 select_n.132
  157.8 0.0 copy-start.2
  157.8 0.5 copy-done.2
  158.4 0.4 fusion.42
  158.7 0.1 pad_maximum_fusion
  158.8 1.3 all_to_all.14
  160.1 5.1 %all-to-all-start = ((f32[128,2,768]{2,1,0:T(2,128)}), f32[128,2,768]{2,1,0:T(2,128)S(1)}, u32[]{:S(2)}, u32[]{:S(2)}) async-start(f32[128,2,768]{2,1,0:T(2,128)} %all_to_all.14), calls=%async_computation | async-start | bytes 1572864 | tf_op jit(solution)/shard_map/all_to_all | solution.py:131
  165.2 0.1 copy.82
  165.4 0.1 cosine_multiply_fusion.3
  165.5 1.9 copy.81
  167.5 0.6 convert_element_type.98
  168.0 0.8 copy.79
  168.8 0.7 reshape.563
  169.5 0.0 copy-start.4
  169.5 12.1 %all-to-all-done = f32[128,2,768]{2,1,0:T(2,128)S(1)} async-done(((f32[128,2,768]{2,1,0:T(2,128)}), f32[128,2,768]{2,1,0:T(2,128)S(1)}, u32[]{:S(2)}, u32[]{:S(2)}) %all-to-all-start) | async-done | bytes 786464 | tf_op jit(solution)/shard_map/all_to_all | solution.py:131
  181.6 1.4 all_to_all.16
  183.0 0.0 copy-start.3
  183.1 1.1 slice_subtract_fusion
  184.1 0.0 copy-done.4
  184.1 1.3 convolution_subtract_fusion
  185.5 0.1 fusion.40
  185.6 0.1 copy.83
  185.7 0.0 copy-done.3
  185.7 0.0 copy-done.5
  185.7 0.6 fusion.31
  186.3 0.1 fusion.37
  186.4 1.3 copy.120
  187.7 0.6 fusion.47
  188.4 2.4 copy.85
  190.8 1.9 fusion.60
  192.7 2.6 copy.86
  195.2 4.9 %all-to-all-start.1 = ((f32[32,128,128]{2,1,0:T(8,128)}), f32[32,128,128]{2,1,0:T(8,128)S(1)}, u32[]{:S(2)}, u32[]{:S(2)}) async-start(f32[32,128,128]{2,1,0:T(8,128)} %copy.86), calls=%async_computation.1 | async-start | bytes 4194304 | tf_op jit(solution)/shard_map/all_to_all | solution.py:39
  200.2 3.5 %cosine_multiply_fusion.2 = f32[512,512]{0,1:T(8,128)S(1)} fusion(f32[512]{0:T(512)S(1)} %get-tuple-element.75, f32[512]{0:T(512)S(1)} %get-tuple-element.76, f32[512]{0:T(512)S(1)} %fusion.63), kind=kLoop, calls=%fused_computation.42 | loop fusion | flops 786432 | bytes 1054720 | tf_op jit(solution)/shard_map/mul | solution.py:16
  203.7 15.1 %cosine_multiply_fusion = f32[1024,1024]{0,1:T(8,128)} fusion(f32[1024]{0:T(1024)S(1)} %get-tuple-element.73, f32[1024]{0:T(1024)S(1)} %get-tuple-element.74, f32[1024]{0:T(1024)S(1)} %fusion.62), kind=kLoop, calls=%fused_computation | loop fusion | flops 3145728 | bytes 4206592 | tf_op jit(solution)/shard_map/mul | solution.py:16
  218.8 11.3 %cosine_multiply_fusion.1 = (f32[1,512,1024]{2,1,0:T(8,128)}, f32[1,512,1024]{2,1,0:T(8,128)}) fusion(f32[1024]{0:T(1024)S(1)} %multiply_multiply_fusion.5, f32[512]{0:T(512)S(1)} %multiply_add_fusion.3), kind=kLoop, calls=%fused_computation.37 | loop fusion | flops 20447232 | bytes 4200448 | tf_op jit(solution)/shard_map/mul | solution.py:73
  230.1 0.0 all-to-all-done.1
  230.1 1.9 fusion.67
  232.1 0.3 copy-done
  232.3 7.0 %fusion.13 = f32[1,512,1024]{2,1,0:T(8,128)S(1)} fusion(f32[1,512,1024]{2,1,0:T(8,128)} %get-tuple-element.72, f32[1,1,512,1024]{3,2,1,0:T(8,128)} %param.15, f32[1,512,1024]{2,1,0:T(8,128)} %get-tuple-element.71, f32[1,1,512,1024]{3,2,1,0:T(8,128)} %param.14, f32[1024,8,128]{0,2,1:T(8,128)S(1)} %bitcast.106, f32[512,8,128,1]{2,0,1,3:T(8,128)S(1)} %fusion.67), kind=kOutput, calls=%fused_computation.22 | convolution fusion | flops 3223322624 | bytes 16777216 | tf_op jit(solution)/shard_map/cjy,bjy->bc/dot_general | solution.py:44
  239.4 0.0 copy-start.1
  239.4 3.5 %fusion.11 = f32[512,8,128]{0,2,1:T(8,128)S(1)} fusion(f32[1024,8,128]{0,2,1:T(8,128)S(1)} %bitcast.107, f32[1,512,1024]{2,1,0:T(8,128)S(1)} %fusion.13), kind=kOutput, calls=%fused_computation.19 | convolution fusion | flops 3221225472 | bytes 8388608 | tf_op jit(solution)/shard_map/cjy,bc->bjy/dot_general | solution.py:54
  242.9 0.0 copy-done.1
  242.9 1.8 fusion.24
  244.8 1.8 copy.93
  246.6 35.6 %all_to_all.22 = f32[32,128,128]{2,1,0:T(8,128)S(1)} all-to-all(f32[32,128,128]{2,1,0:T(8,128)} %bitcast.112), channel_id=1, replica_groups=mesh['grp'=4,'gx'=4,'gy'=8] {'gx','gy'}, dimensions={0} | all-to-all | bytes 4194304 | tf_op jit(solution)/shard_map/all_to_all | solution.py:57
  282.2 3.0 %fusion.21 = f32[1,32,128,128]{3,1,2,0:T(8,128)S(1)} fusion(f32[32,128,128]{2,1,0:T(8,128)S(1)} %all_to_all.22, f32[32,32]{0,1:T(8,128)S(1)} %cosine_multiply_fusion.3), kind=kOutput, calls=%fused_computation.39 | convolution fusion | flops 201326592 | bytes 4198400 | tf_op jit(solution)/shard_map/kz,kxy->zxy/dot_general | solution.py:58
  285.2 2.5 copy.95
  (18 shorter events, 0.1 us)
Async XLA Ops:
  7.2 3.9 %slice-start = ((f32[1,32,128,128]{3,2,1,0:T(8,128)}), f32[1,3,128,128]{3,2,1,0:T(8,128)S(1)}, s32[]{:S(2)}) async-start(f32[1,32,128,128]{3,2,1,0:T(8,128)} %param.16), calls=%async_computation.4 | async-start | bytes 393216 | tf_op jit(solution)/shard_map/slice | solution.py:112
  7.2 149.1 %all-reduce.2.cloned.1.call-start = ((), (), s32[]{:S(2)}) async-start(), calls=%async_computation.3 | async-start | bytes 131072 | tf_op jit(solution)/shard_map/psum | solution.py:120
  157.8 0.5 copy-start.2
  160.1 21.5 %all-to-all-start = ((f32[128,2,768]{2,1,0:T(2,128)}), f32[128,2,768]{2,1,0:T(2,128)S(1)}, u32[]{:S(2)}, u32[]{:S(2)}) async-start(f32[128,2,768]{2,1,0:T(2,128)} %all_to_all.14), calls=%async_computation | async-start | bytes 1572864 | tf_op jit(solution)/shard_map/all_to_all | solution.py:131
  169.5 14.6 %copy-start.4 = (s32[1,128,1]{1,2,0:T(1,128)S(1)}, s32[1,128,1]{1,2,0:T(1,128)}, u32[]{:S(2)}) copy-start(s32[1,128,1]{1,2,0:T(1,128)} %param.18) | copy-start | bytes 1540
  183.0 2.7 copy-start.3
  183.1 2.7 copy-start.5
  195.2 34.9 %all-to-all-start.1 = ((f32[32,128,128]{2,1,0:T(8,128)}), f32[32,128,128]{2,1,0:T(8,128)S(1)}, u32[]{:S(2)}, u32[]{:S(2)}) async-start(f32[32,128,128]{2,1,0:T(8,128)} %copy.86), calls=%async_computation.1 | async-start | bytes 4194304 | tf_op jit(solution)/shard_map/all_to_all | solution.py:39
  230.1 2.2 copy-start
  239.4 3.6 %copy-start.1 = (f32[1,512,1024]{2,1,0:T(8,128)}, f32[1,512,1024]{2,1,0:T(8,128)S(1)}, u32[]{:S(2)}) copy-start(f32[1,512,1024]{2,1,0:T(8,128)S(1)} %fusion.13) | copy-start | bytes 6291460
Sparse Core Ops, SparseCore 0:
  13.3 142.9 all-reduce.1
where the time goes:
time: 295 us
  waiting for transfers between devices  157 us (53%)
  blocking collectives  35.6 us (12%)
  other arithmetic  35.3 us (12%)
  matrix products  22.6 us (8%)
  local copies, waits for them, and re-layouts  19.4 us (7%)
  between operations  14.4 us (5%)
  starting transfers between devices  10 us (3%)
    psum x1, waiting for transfers between devices, shards(): codes = lax.psum(jnp.where(owner, mine[None, :], 0.0), every)  145 us
    all_to_all x1, blocking collectives, to_cells(): lax.all_to_all(part, ('gx', 'gy'), split_axis=0, concat_axis=0, tiled=True)  35.6 us
    mul x4, other arithmetic, cosine_table(): return scale * jnp.cos(jnp.pi * rows * (cols + 0.5) / count)  18.7 us
    all_to_all x1, waiting for transfers between devices, shards(): lax.all_to_all(jnp.concatenate([rims_out, met], axis=1), every, split_axi...  12.1 us
    mul x1, other arithmetic, advance_terms(): return (2.0 * jnp.cos(theta), COURANT * COURANT * shape * shape)  11.3 us
    dot_general x1, matrix products, to_modes(): return jnp.einsum('cjy,bjy->bc', split_y, part, precision=FAST)[None, None]  7.03 us
    unnamed x19, local copies, waits for them, and re-layouts  7.02 us
  transfers between devices with their start and end apart: 3, of which 2 were waited for; matrix products, arithmetic and copies ran while one was open for 12% of the time, Pallas kernels for 0%

commit v1 on v0

--- a/solution.py
+++ b/solution.py
@@ -117,7 +117,8 @@
     slots = strip_slot.reshape(-1)
     mine = (slots * rows_x + strip_row.reshape(-1)).astype(jnp.float32)
     owner = jnp.arange(devices, dtype=jnp.int32)[:, None] == lax.axis_index(every)
-    codes = lax.psum(jnp.where(owner, mine[None, :], 0.0), every)
+    z_in = jnp.where(owner, mine[None, :], 0.0)
+    codes = lax.all_gather(z_in, every).sum(axis=0)
     codes = jnp.round(codes).astype(jnp.int32)
     want = lax.axis_index(every) * slots_per + jnp.arange(slots_per, dtype=jnp.int32)
     hit = (codes // rows_x)[:, :, None] == want[None, None, :]

time: 295 us -> 227 us (0.77)
  waiting for transfers between devices: 157 us -> 85.5 us
  other arithmetic: 35.3 us -> 38.3 us
    psum x1 -> x0, waiting for transfers between devices: 145 us -> none  [shards(): codes = lax.psum(jnp.where(owner, mine[None, :], 0.0), every)]
    all_gather x0 -> x1, waiting for transfers between devices: none -> 73.4 us  [shards(): codes = lax.all_gather(z_in, every).sum(axis=0)]
    reduce_sum x0 -> x1, other arithmetic: none -> 3.81 us  [shards(): codes = lax.all_gather(z_in, every).sum(axis=0)]
    unnamed x19 -> x21, local copies, waits for them, and re-layouts: 7.02 us -> 7.02 us
  transfers between devices with their start and end apart: 3 -> 3, of which waited for: 2 -> 2; matrix products, arithmetic and copies ran while one was open for 12% -> 16% of each run, Pallas kernels for 0% -> 0%
where the time goes in v1:
time: 227 us; the launch traced here: 226 us
  waiting for transfers between devices  85.5 us (38%)
  other arithmetic  38.3 us (17%)
  blocking collectives  35.6 us (16%)
  matrix products  21.9 us (10%)
  local copies, waits for them, and re-layouts  20.4 us (9%)
  between operations  14.4 us (6%)
  starting transfers between devices  10.3 us (5%)
    all_gather x1, waiting for transfers between devices, shards(): codes = lax.all_gather(z_in, every).sum(axis=0)  73.4 us
    all_to_all x1, blocking collectives, to_cells(): lax.all_to_all(part, ('gx', 'gy'), split_axis=0, concat_axis=0, tiled=True)  35.6 us
    mul x4, other arithmetic, cosine_table(): return scale * jnp.cos(jnp.pi * rows * (cols + 0.5) / count)  18.7 us
    all_to_all x1, waiting for transfers between devices, shards(): lax.all_to_all(jnp.concatenate([rims_out, met], axis=1), every, split_axi...  12.1 us
    mul x1, other arithmetic, advance_terms(): return (2.0 * jnp.cos(theta), COURANT * COURANT * shape * shape)  11.3 us
    dot_general x1, matrix products, to_modes(): return jnp.einsum('cjy,bjy->bc', split_y, part, precision=FAST)[None, None]  7.03 us
    unnamed x21, local copies, waits for them, and re-layouts  7.02 us
    all_to_all x1, starting transfers between devices, shards(): lax.all_to_all(jnp.concatenate([rims_out, met], axis=1), every, split_axi...  5.35 us
  transfers between devices with their start and end apart: 3, of which 2 were waited for; matrix products, arithmetic and copies ran while one was open for 16% of the time, Pallas kernels for 0%

profile of v1, /device:TPU:1, one launch (start us, length us, event | category | flops | bytes accessed | tf_op | source)
XLA Modules:
  0.0 226.4 jit_solution(3146035619721594867)
XLA Ops:
  7.2 0.0 copy-start.4
  7.2 0.0 all-gather.2.cloned.1.call-start
  7.2 0.7 fusion.64
  7.9 0.7 broadcast_select_fusion
  8.6 0.0 all-gather.2.cloned.1.call-update
  8.7 0.9 slice.156
  9.6 0.1 copy.108
  9.7 0.9 fusion.66
  10.7 0.1 copy.109
  10.8 0.1 copy.110
  10.9 0.1 copy.111
  11.0 0.0 copy-done.4
  11.0 0.4 fusion.43
  11.4 73.4 %all-gather.2.cloned.1.call-done = f32[128,128,128]{2,1,0:T(8,128)} async-done(((f32[1,128,128]{2,1,0:T(8,128)}), f32[128,128,128]{2,1,0:T(8,128)}) %all-gather.2.cloned.1.call-update) | async-done | bytes 8388624 | tf_op jit(solution)/shard_map/all_gather | solution.py:121
  84.8 3.8 %reduce_sum.18 = f32[128,128]{1,0:T(8,128)S(1)} reduce(f32[128,128,128]{2,1,0:T(8,128)} %all-gather.2.cloned.1.call-done, f32[]{:T(128)} %constant.223.clone.1), dimensions={0}, to_apply=%region_0.1 | reduce | flops 2080768 | bytes 8454148 | tf_op jit(solution)/shard_map/reduce_sum | solution.py:121
  88.6 0.1 add_select_fusion
  88.7 0.2 compare_reduce_fusion
  88.9 0.2 fusion.39
  89.1 0.1 copy.74
  89.2 0.1 select_n.147
  89.3 0.0 copy-start.2
  89.3 0.5 copy-done.2
  89.9 0.4 fusion.42
  90.2 0.1 pad_maximum_fusion
  90.3 1.3 all_to_all.14
  91.6 5.4 %all-to-all-start = ((f32[128,2,768]{2,1,0:T(2,128)}), f32[128,2,768]{2,1,0:T(2,128)S(1)}, u32[]{:S(2)}, u32[]{:S(2)}) async-start(f32[128,2,768]{2,1,0:T(2,128)} %all_to_all.14), calls=%async_computation | async-start | bytes 1572864 | tf_op jit(solution)/shard_map/all_to_all | solution.py:132
  97.0 0.1 copy.82
  97.2 0.1 cosine_multiply_fusion.3
  97.3 1.9 copy.81
  99.2 0.6 convert_element_type.105
  99.8 0.8 copy.79
  100.6 0.7 reshape.636
  101.3 12.1 %all-to-all-done = f32[128,2,768]{2,1,0:T(2,128)S(1)} async-done(((f32[128,2,768]{2,1,0:T(2,128)}), f32[128,2,768]{2,1,0:T(2,128)S(1)}, u32[]{:S(2)}, u32[]{:S(2)}) %all-to-all-start) | async-done | bytes 786464 | tf_op jit(solution)/shard_map/all_to_all | solution.py:132
  113.4 1.4 all_to_all.16
  114.8 1.1 slice_subtract_fusion
  115.9 0.0 copy-done.5
  115.9 1.3 convolution_subtract_fusion
  117.2 0.1 fusion.40
  117.3 0.1 copy.83
  117.5 0.0 copy-done.3
  117.5 0.0 copy-done.6
  117.5 0.6 fusion.31
  118.1 0.1 fusion.37
  118.2 1.3 copy.119
  119.5 0.6 fusion.47
  120.1 2.4 %copy.85 = f32[32,128,128]{2,0,1:T(8,128)S(1)} copy(f32[32,128,128]{1,2,0:T(8,128)} %fusion.47) | data formatting | bytes 4194304 | tf_op jit(solution)/shard_map/scatter-add | solution.py:145
  122.5 1.9 fusion.60
  124.4 2.6 %copy.86 = f32[32,128,128]{2,1,0:T(8,128)} copy(f32[32,128,128]{2,0,1:T(8,128)S(1)} %fusion.60) | data formatting | bytes 4194304 | tf_op jit(solution)/shard_map/kz,zxy->kxy/dot_general | solution.py:38
  127.0 4.9 %all-to-all-start.1 = ((f32[32,128,128]{2,1,0:T(8,128)}), f32[32,128,128]{2,1,0:T(8,128)S(1)}, u32[]{:S(2)}, u32[]{:S(2)}) async-start(f32[32,128,128]{2,1,0:T(8,128)} %copy.86), calls=%async_computation.1 | async-start | bytes 4194304 | tf_op jit(solution)/shard_map/all_to_all | solution.py:39
  131.9 3.5 %cosine_multiply_fusion.2 = f32[512,512]{0,1:T(8,128)S(1)} fusion(f32[512]{0:T(512)S(1)} %get-tuple-element.75, f32[512]{0:T(512)S(1)} %get-tuple-element.76, f32[512]{0:T(512)S(1)} %fusion.63), kind=kLoop, calls=%fused_computation.42 | loop fusion | flops 786432 | bytes 1054720 | tf_op jit(solution)/shard_map/mul | solution.py:16
  135.5 15.1 %cosine_multiply_fusion = f32[1024,1024]{0,1:T(8,128)} fusion(f32[1024]{0:T(1024)S(1)} %get-tuple-element.73, f32[1024]{0:T(1024)S(1)} %get-tuple-element.74, f32[1024]{0:T(1024)S(1)} %fusion.62), kind=kLoop, calls=%fused_computation | loop fusion | flops 3145728 | bytes 4206592 | tf_op jit(solution)/shard_map/mul | solution.py:16
  150.5 11.3 %cosine_multiply_fusion.1 = (f32[1,512,1024]{2,1,0:T(8,128)}, f32[1,512,1024]{2,1,0:T(8,128)}) fusion(f32[1024]{0:T(1024)S(1)} %multiply_multiply_fusion.5, f32[512]{0:T(512)S(1)} %multiply_add_fusion.3), kind=kLoop, calls=%fused_computation.37 | loop fusion | flops 20447232 | bytes 4200448 | tf_op jit(solution)/shard_map/mul | solution.py:73
  161.9 0.0 all-to-all-done.1
  161.9 1.9 fusion.67
  163.8 0.3 copy-done
  164.1 7.0 %fusion.13 = f32[1,512,1024]{2,1,0:T(8,128)S(1)} fusion(f32[1,512,1024]{2,1,0:T(8,128)} %get-tuple-element.72, f32[1,1,512,1024]{3,2,1,0:T(8,128)} %param.15, f32[1,512,1024]{2,1,0:T(8,128)} %get-tuple-element.71, f32[1,1,512,1024]{3,2,1,0:T(8,128)} %param.14, f32[1024,8,128]{0,2,1:T(8,128)S(1)} %bitcast.106, f32[512,8,128,1]{2,0,1,3:T(8,128)S(1)} %fusion.67), kind=kOutput, calls=%fused_computation.22 | convolution fusion | flops 3223322624 | bytes 16777216 | tf_op jit(solution)/shard_map/cjy,bjy->bc/dot_general | solution.py:44
  171.1 0.0 copy-start.1
  171.1 3.5 %fusion.11 = f32[512,8,128]{0,2,1:T(8,128)S(1)} fusion(f32[1024,8,128]{0,2,1:T(8,128)S(1)} %bitcast.107, f32[1,512,1024]{2,1,0:T(8,128)S(1)} %fusion.13), kind=kOutput, calls=%fused_computation.19 | convolution fusion | flops 3221225472 | bytes 8388608 | tf_op jit(solution)/shard_map/cjy,bc->bjy/dot_general | solution.py:54
  174.7 0.0 copy-done.1
  174.7 1.8 fusion.24
  176.5 1.8 copy.93
  178.3 35.6 %all_to_all.22 = f32[32,128,128]{2,1,0:T(8,128)S(1)} all-to-all(f32[32,128,128]{2,1,0:T(8,128)} %bitcast.112), channel_id=1, replica_groups=mesh['grp'=4,'gx'=4,'gy'=8] {'gx','gy'}, dimensions={0} | all-to-all | bytes 4194304 | tf_op jit(solution)/shard_map/all_to_all | solution.py:57
  214.0 3.0 %fusion.21 = f32[1,32,128,128]{3,1,2,0:T(8,128)S(1)} fusion(f32[32,128,128]{2,1,0:T(8,128)S(1)} %all_to_all.22, f32[32,32]{0,1:T(8,128)S(1)} %cosine_multiply_fusion.3), kind=kOutput, calls=%fused_computation.39 | convolution fusion | flops 201326592 | bytes 4198400 | tf_op jit(solution)/shard_map/kz,kxy->zxy/dot_general | solution.py:58
  217.0 2.5 %copy.95 = f32[1,32,128,128]{3,2,1,0:T(8,128)} copy(f32[1,32,128,128]{3,1,2,0:T(8,128)S(1)} %fusion.21) | data formatting | bytes 4194304
  (20 shorter events, 0.2 us)
Async XLA Ops:
  7.2 3.8 %copy-start.4 = (s32[1,128,1]{1,2,0:T(1,128)S(1)}, s32[1,128,1]{1,2,0:T(1,128)}, u32[]{:S(2)}) copy-start(s32[1,128,1]{1,2,0:T(1,128)} %param.18) | copy-start | bytes 1540
  7.2 77.7 %all-gather.2.cloned.1.call-start = ((), (), s32[]{:S(2)}) async-start(), calls=%async_computation.3 | async-start | bytes 8454144 | tf_op jit(solution)/shard_map/all_gather | solution.py:121
  89.3 0.5 copy-start.2
  91.6 21.7 %all-to-all-start = ((f32[128,2,768]{2,1,0:T(2,128)}), f32[128,2,768]{2,1,0:T(2,128)S(1)}, u32[]{:S(2)}, u32[]{:S(2)}) async-start(f32[128,2,768]{2,1,0:T(2,128)} %all_to_all.14), calls=%async_computation | async-start | bytes 1572864 | tf_op jit(solution)/shard_map/all_to_all | solution.py:132
  101.3 14.6 %copy-start.5 = (s32[1,128,1]{1,2,0:T(1,128)S(1)}, s32[1,128,1]{1,2,0:T(1,128)}, u32[]{:S(2)}) copy-start(s32[1,128,1]{1,2,0:T(1,128)} %param.18) | copy-start | bytes 1540
  114.8 2.7 %copy-start.3 = (s32[256]{0:T(256)S(1)}, s32[256]{0:T(256)}, u32[]{:S(2)}) copy-start(s32[256]{0:T(256)} %copy-done.2) | copy-start | bytes 3076
  114.8 2.7 %copy-start.6 = (f32[256]{0:T(256)S(1)}, f32[256]{0:T(256)}, u32[]{:S(2)}) copy-start(f32[256]{0:T(256)} %reshape.636) | copy-start | bytes 3076
  127.0 34.9 %all-to-all-start.1 = ((f32[32,128,128]{2,1,0:T(8,128)}), f32[32,128,128]{2,1,0:T(8,128)S(1)}, u32[]{:S(2)}, u32[]{:S(2)}) async-start(f32[32,128,128]{2,1,0:T(8,128)} %copy.86), calls=%async_computation.1 | async-start | bytes 4194304 | tf_op jit(solution)/shard_map/all_to_all | solution.py:39
  161.9 2.2 copy-start
  171.1 3.6 %copy-start.1 = (f32[1,512,1024]{2,1,0:T(8,128)}, f32[1,512,1024]{2,1,0:T(8,128)S(1)}, u32[]{:S(2)}) copy-start(f32[1,512,1024]{2,1,0:T(8,128)S(1)} %fusion.13) | copy-start | bytes 6291460
Sparse Core Ops, SparseCore 0:
  11.5 73.2 all-gather.1
